TPU v7x, 256 devices: a whole 4x4x8 slice. The times are simulated.
256 devices in a mesh: vgrp: 4 (over y), samp: 64 (over z, x, core).
Axes of the slice: x: 4, y: 4, z: 8, core: 2. Of those that a mesh axis runs over, the one named last changes fastest.
Arguments:
- phenotype: float32 [196608], P(('vgrp', 'samp')), may hold values from -6 to 6
- exposures: float32 [196608, 128], P('samp'), may hold values from -6 to 6
- perms: int32 [16, 196608], P(None, 'samp'), may hold values from 0 to 196607, each once within a row
- genotypes: int32 [196608, 2048], P('samp', 'vgrp'), may hold values from 0 to 2
Outputs:
- statistics: float32 [2048, 16], P(('vgrp', 'samp'))
Inputs may be any that keep to these rules, and one draw needn't show every extreme that they name: Each row of perms holds every sample index once.
All inputs are finite; a program needn't handle non-finite values.
Results may differ from a plain program's by a relative error of at most 0.00075.
Values sent between devices are 32-bit elements; how exact they have to be, the bound alone decides.
No kernel may reach another device: no remote copies, remote signals or barrier semaphores. Data moves between devices by JAX's collectives and lax.ppermute only.
A program may use at most 64 MiB of HBM per device.

v0:
```python
import jax
import jax.numpy as jnp
from jax import lax
from jax.sharding import PartitionSpec as P


def chol_solve(factor, rhs):
    middle = lax.linalg.triangular_solve(factor, rhs, left_side=True, lower=True)
    return lax.linalg.triangular_solve(factor, middle, left_side=True, lower=True, transpose_a=True)


def permute_rows(pheno_full, perms):
    samples = pheno_full.shape[0]
    table = pheno_full.reshape(samples // 128, 128)
    lanes = lax.broadcasted_iota(jnp.int32, (1, 128), 1)

    def one_perm(index_row):
        picked_rows = table[index_row // 128]
        wanted = (index_row % 128)[:, None] == lanes
        return jnp.sum(jnp.where(wanted, picked_rows, jnp.float32(0.0)), axis=1)

    return lax.map(one_perm, perms)


def per_device(phenotype, exposures, perms, genotypes):
    hi = lax.Precision.HIGHEST
    pheno_full = lax.all_gather(phenotype, ("vgrp", "samp"), axis=0, tiled=True)
    samples = pheno_full.shape[0]
    local_rows = exposures.shape[0]
    width = exposures.shape[1]
    quarter = local_rows // lax.axis_size("vgrp")
    offset_rows = lax.axis_index("vgrp") * quarter
    perm_rows = permute_rows(pheno_full, perms)
    expo_part = lax.dynamic_slice_in_dim(exposures, offset_rows, quarter, 0)
    pheno_part = lax.dynamic_slice_in_dim(perm_rows, offset_rows, quarter, 1)
    gram_part = jnp.dot(expo_part.T, expo_part, precision=hi)
    cross_part = jnp.dot(expo_part.T, pheno_part.T, precision=hi)
    gram, cross = lax.psum((gram_part, cross_part), ("vgrp", "samp"))
    system = gram + 0.5 * samples * jnp.eye(width, dtype=jnp.float32)
    factor = jnp.linalg.cholesky(system)
    coefficients = chol_solve(factor, cross)
    permuted = jnp.transpose(perm_rows)
    residuals = permuted - jnp.dot(exposures, coefficients, precision=hi)
    nperm = residuals.shape[1]
    weighted = (
        (exposures[:, :, None] * residuals[:, None, :])
        .reshape(local_rows, width * nperm)
        .astype(jnp.bfloat16)
    )
    dosages = genotypes.astype(jnp.bfloat16)
    own_rows = genotypes.shape[1] // lax.axis_size("samp")
    summed = lax.psum(jnp.dot(dosages.T, weighted, preferred_element_type=jnp.float32), "samp")
    own_scores = lax.dynamic_slice_in_dim(summed, lax.axis_index("samp") * own_rows, own_rows, 0)
    shaped = own_scores.reshape(own_rows, width, nperm)
    return jnp.sum(shaped * shaped, axis=1) / (samples * width)


def solution(mesh):
    return jax.shard_map(
        per_device,
        mesh=mesh,
        in_specs=(P(("vgrp", "samp")), P("samp", None), P(None, "samp"), P("samp", "vgrp")),
        out_specs=P(("vgrp", "samp"), None),
        check_vma=False,
    )
```

profile of v0, /device:TPU:8, one launch (start us, length us, event | category | flops | bytes accessed | tf_op | source)
XLA Modules:
  0.0 587.2 jit_solution(16091386227517214379)
XLA Ops:
  6.5 2.6 fusion.7
  9.9 77.2 %all-gather = f32[256,1,768]{2,1,0:T(1,128)S(1)} all-gather(f32[1,1,768]{2,1,0:T(1,128)S(1)} %reshape.133), channel_id=1, replica_groups=mesh['vgrp'=4,'samp'=64] {'vgrp','samp'}, dimensions={0}, use_global_device_ids=true | all-gather | bytes 789504 | tf_op jit(solution)/shard_map/all_gather | solution.py:27
  87.0 181.6 %while.13 = (s32[]{:T(128)}, f32[16,3072]{1,0:T(8,128)S(1)}, s32[16,3072]{1,0:T(8,128)}, f32[1536,128]{1,0:T(8,128)S(1)}, s32[]{:T(128)}, /*index=5*/s32[]{:T(128)}) while((s32[]{:T(128)}, f32[16,3072]{1,0:T(8,128)S(1)}, s32[16,3072]{1,0:T(8,128)}, f32[1536,128]{1,0:T(8,128)S(1)}, s32[]{:T(128)}, /*index=5*/s32[]{:T(128)}) %tuple.39), condition=%wide.region_2.3_spmd.clone, body=%wide.region_0.2_spmd.clone.sunk | while | flops 1268738 | bytes 4866133 | solution.py:22
  88.0 8.1 %gather_fusion = f32[3072,128]{1,0:T(8,128)S(1)} fusion(f32[1536,128]{1,0:T(8,128)S(1)} %get-tuple-element.138, s32[3072]{0:T(1024)S(1)} %broadcast_clamp_fusion.2), kind=kCustom, calls=%fused_computation.clone.clone.1 | custom fusion | bytes 3158016 | tf_op jit(solution)/shard_map/while/body/eval_jaxpr/gather | solution.py:18
  96.2 1.9 select_reduce_fusion.3
  99.4 8.1 %gather_fusion = f32[3072,128]{1,0:T(8,128)S(1)} fusion(f32[1536,128]{1,0:T(8,128)S(1)} %get-tuple-element.138, s32[3072]{0:T(1024)S(1)} %broadcast_clamp_fusion.2), kind=kCustom, calls=%fused_computation.clone.clone.1 | custom fusion | bytes 3158016 | tf_op jit(solution)/shard_map/while/body/eval_jaxpr/gather | solution.py:18
  107.5 1.9 select_reduce_fusion.3
  110.7 8.1 %gather_fusion = f32[3072,128]{1,0:T(8,128)S(1)} fusion(f32[1536,128]{1,0:T(8,128)S(1)} %get-tuple-element.138, s32[3072]{0:T(1024)S(1)} %broadcast_clamp_fusion.2), kind=kCustom, calls=%fused_computation.clone.clone.1 | custom fusion | bytes 3158016 | tf_op jit(solution)/shard_map/while/body/eval_jaxpr/gather | solution.py:18
  122.1 8.1 %gather_fusion = f32[3072,128]{1,0:T(8,128)S(1)} fusion(f32[1536,128]{1,0:T(8,128)S(1)} %get-tuple-element.138, s32[3072]{0:T(1024)S(1)} %broadcast_clamp_fusion.2), kind=kCustom, calls=%fused_computation.clone.clone.1 | custom fusion | bytes 3158016 | tf_op jit(solution)/shard_map/while/body/eval_jaxpr/gather | solution.py:18
  133.4 8.1 %gather_fusion = f32[3072,128]{1,0:T(8,128)S(1)} fusion(f32[1536,128]{1,0:T(8,128)S(1)} %get-tuple-element.138, s32[3072]{0:T(1024)S(1)} %broadcast_clamp_fusion.2), kind=kCustom, calls=%fused_computation.clone.clone.1 | custom fusion | bytes 3158016 | tf_op jit(solution)/shard_map/while/body/eval_jaxpr/gather | solution.py:18
  141.6 1.9 select_reduce_fusion.3
  144.8 8.1 %gather_fusion = f32[3072,128]{1,0:T(8,128)S(1)} fusion(f32[1536,128]{1,0:T(8,128)S(1)} %get-tuple-element.138, s32[3072]{0:T(1024)S(1)} %broadcast_clamp_fusion.2), kind=kCustom, calls=%fused_computation.clone.clone.1 | custom fusion | bytes 3158016 | tf_op jit(solution)/shard_map/while/body/eval_jaxpr/gather | solution.py:18
  156.1 8.1 %gather_fusion = f32[3072,128]{1,0:T(8,128)S(1)} fusion(f32[1536,128]{1,0:T(8,128)S(1)} %get-tuple-element.138, s32[3072]{0:T(1024)S(1)} %broadcast_clamp_fusion.2), kind=kCustom, calls=%fused_computation.clone.clone.1 | custom fusion | bytes 3158016 | tf_op jit(solution)/shard_map/while/body/eval_jaxpr/gather | solution.py:18
  167.5 8.1 %gather_fusion = f32[3072,128]{1,0:T(8,128)S(1)} fusion(f32[1536,128]{1,0:T(8,128)S(1)} %get-tuple-element.138, s32[3072]{0:T(1024)S(1)} %broadcast_clamp_fusion.2), kind=kCustom, calls=%fused_computation.clone.clone.1 | custom fusion | bytes 3158016 | tf_op jit(solution)/shard_map/while/body/eval_jaxpr/gather | solution.py:18
  175.6 1.9 select_reduce_fusion.3
  178.8 8.1 %gather_fusion = f32[3072,128]{1,0:T(8,128)S(1)} fusion(f32[1536,128]{1,0:T(8,128)S(1)} %get-tuple-element.138, s32[3072]{0:T(1024)S(1)} %broadcast_clamp_fusion.2), kind=kCustom, calls=%fused_computation.clone.clone.1 | custom fusion | bytes 3158016 | tf_op jit(solution)/shard_map/while/body/eval_jaxpr/gather | solution.py:18
  187.0 1.9 select_reduce_fusion.3
  190.2 8.1 %gather_fusion = f32[3072,128]{1,0:T(8,128)S(1)} fusion(f32[1536,128]{1,0:T(8,128)S(1)} %get-tuple-element.138, s32[3072]{0:T(1024)S(1)} %broadcast_clamp_fusion.2), kind=kCustom, calls=%fused_computation.clone.clone.1 | custom fusion | bytes 3158016 | tf_op jit(solution)/shard_map/while/body/eval_jaxpr/gather | solution.py:18
  198.3 1.9 select_reduce_fusion.3
  201.6 8.1 %gather_fusion = f32[3072,128]{1,0:T(8,128)S(1)} fusion(f32[1536,128]{1,0:T(8,128)S(1)} %get-tuple-element.138, s32[3072]{0:T(1024)S(1)} %broadcast_clamp_fusion.2), kind=kCustom, calls=%fused_computation.clone.clone.1 | custom fusion | bytes 3158016 | tf_op jit(solution)/shard_map/while/body/eval_jaxpr/gather | solution.py:18
  212.9 8.1 %gather_fusion = f32[3072,128]{1,0:T(8,128)S(1)} fusion(f32[1536,128]{1,0:T(8,128)S(1)} %get-tuple-element.138, s32[3072]{0:T(1024)S(1)} %broadcast_clamp_fusion.2), kind=kCustom, calls=%fused_computation.clone.clone.1 | custom fusion | bytes 3158016 | tf_op jit(solution)/shard_map/while/body/eval_jaxpr/gather | solution.py:18
  224.3 8.1 %gather_fusion = f32[3072,128]{1,0:T(8,128)S(1)} fusion(f32[1536,128]{1,0:T(8,128)S(1)} %get-tuple-element.138, s32[3072]{0:T(1024)S(1)} %broadcast_clamp_fusion.2), kind=kCustom, calls=%fused_computation.clone.clone.1 | custom fusion | bytes 3158016 | tf_op jit(solution)/shard_map/while/body/eval_jaxpr/gather | solution.py:18
  235.6 8.1 %gather_fusion = f32[3072,128]{1,0:T(8,128)S(1)} fusion(f32[1536,128]{1,0:T(8,128)S(1)} %get-tuple-element.138, s32[3072]{0:T(1024)S(1)} %broadcast_clamp_fusion.2), kind=kCustom, calls=%fused_computation.clone.clone.1 | custom fusion | bytes 3158016 | tf_op jit(solution)/shard_map/while/body/eval_jaxpr/gather | solution.py:18
  247.0 8.1 %gather_fusion = f32[3072,128]{1,0:T(8,128)S(1)} fusion(f32[1536,128]{1,0:T(8,128)S(1)} %get-tuple-element.138, s32[3072]{0:T(1024)S(1)} %broadcast_clamp_fusion.2), kind=kCustom, calls=%fused_computation.clone.clone.1 | custom fusion | bytes 3158016 | tf_op jit(solution)/shard_map/while/body/eval_jaxpr/gather | solution.py:18
  258.3 8.1 %gather_fusion = f32[3072,128]{1,0:T(8,128)S(1)} fusion(f32[1536,128]{1,0:T(8,128)S(1)} %get-tuple-element.138, s32[3072]{0:T(1024)S(1)} %broadcast_clamp_fusion.2), kind=kCustom, calls=%fused_computation.clone.clone.1 | custom fusion | bytes 3158016 | tf_op jit(solution)/shard_map/while/body/eval_jaxpr/gather | solution.py:18
  270.0 2.0 copy.12
  272.0 74.0 %psum.22 = f32[128,16]{0,1:T(8,128)S(1)} all-reduce(f32[128,16]{0,1:T(8,128)S(1)} %fusion.5), channel_id=1, replica_groups=mesh['vgrp'=4,'samp'=64] {'vgrp','samp'}, use_global_device_ids=true, to_apply=%region_6.7 | all-reduce | flops 2048 | bytes 16384 | tf_op jit(solution)/shard_map/psum | solution.py:38
  347.8 11.7 %cholesky.16 = f32[128,128]{1,0:T(8,128)S(1)} custom-call(f32[128,128]{1,0:T(8,128)S(1)} %fusion.14), custom_call_target="Cholesky" | custom-call | tf_op jit(solution)/shard_map/jit(cholesky)/cholesky | solution.py:40
  360.9 9.8 %custom-call.8 = f32[1,128,128]{1,2,0:T(8,128)S(1)} custom-call(f32[1,128,128]{2,1,0:T(8,128)S(1)} %fusion.9), custom_call_target="InvertDiagBlocksLowerTriangular" | custom-call | tf_op jit(solution)/shard_map/triangular_solve | solution.py:9
  372.5 3.4 multiply_convert_fusion
  376.0 8.9 %convolution_bitcast_fusion = f32[512,2048]{0,1:T(8,128)} fusion(bf16[3072,2048]{0,1:T(8,128)(2,1)S(1)} %bitcast.45, s32[3072,512]{1,0:T(8,128)S(1)} %bitcast.51), kind=kOutput, calls=%fused_computation.19 | convolution fusion | flops 6444023808 | bytes 23068672 | tf_op jit(solution)/shard_map/dot_general | solution.py:52
  384.9 193.0 %all-reduce.5.cloned.1.call-done = f32[512,2048]{0,1:T(8,128)} async-done(((f32[512,2048]{0,1:T(8,128)}), f32[512,2048]{0,1:T(8,128)}) %all-reduce.5.cloned.1.call-update) | async-done | bytes 4194320 | tf_op jit(solution)/shard_map/psum | solution.py:52
  (102 shorter events, 48.9 us)
Async XLA Ops:
  6.5 339.5 %all-reduce.3.cloned.1.call-start = ((), (), s32[]{:S(2)}) async-start(), calls=%async_computation | async-start | bytes 131072 | tf_op jit(solution)/shard_map/psum | solution.py:38
  9.1 568.9 %all-reduce.5.cloned.1.call-start = ((), (), s32[]{:S(2)}) async-start(), calls=%async_computation.1 | async-start | bytes 8388608 | tf_op jit(solution)/shard_map/psum | solution.py:52
  270.0 101.1 %copy-start = (f32[3072,128]{1,0:T(8,128)S(1)}, f32[3072,128]{1,0:T(8,128)}, u32[]{:S(2)}) copy-start(f32[3072,128]{1,0:T(8,128)} %param.7) | copy-start | bytes 4718596
  371.1 4.9 slice-start
  372.5 3.5 slice-start.1
Sparse Core Ops, SparseCore 0:
  12.8 243.6 all-reduce.2
  385.1 192.8 all-reduce.4
where the time goes:
time: 588 us; the launch traced here: 587 us
  waiting for transfers between devices  193 us (33%)
  blocking collectives  151 us (26%)
  local copies, waits for them, and re-layouts  138 us (23%)
  other arithmetic  76.4 us (13%)
  matrix products  14.5 us (2%)
  between operations  13.5 us (2%)
    psum x1, waiting for transfers between devices, per_device(): lax.psum(jnp.dot(dosages.T, weighted, preferred_element_type=jnp.float32)...  193 us
    gather x16, local copies, waits for them, and re-layouts, one_perm(): picked_rows = table[index_row // 128]  130 us
    all_gather x1, blocking collectives, per_device(): pheno_full = lax.all_gather(phenotype, ('vgrp', 'samp'), axis=0, tiled=True)  77.2 us
    psum x1, blocking collectives, per_device(): gram, cross = lax.psum((gram_part, cross_part), ('vgrp', 'samp'))  74 us
    reduce_sum x16, other arithmetic, one_perm(): return jnp.sum(jnp.where(wanted, picked_rows, jnp.float32(0.0)), axis=1)  30.2 us
    select_n x16, other arithmetic, one_perm(): picked_rows = table[index_row // 128]  15.6 us
    another operation x3, other arithmetic, per_device(): factor = jnp.linalg.cholesky(system)  12.4 us
  transfers between devices with their start and end apart: 2, of which 1 were waited for; matrix products, arithmetic and copies ran while one was open for 31% of the time, Pallas kernels for 0%

commit v1 on v0

--- a/solution.py
+++ b/solution.py
@@ -24,7 +24,12 @@
 
 def per_device(phenotype, exposures, perms, genotypes):
     hi = lax.Precision.HIGHEST
-    pheno_full = lax.all_gather(phenotype, ("vgrp", "samp"), axis=0, tiled=True)
+    pheno_full = jnp.concatenate(
+        lax.all_to_all(
+            jnp.stack([phenotype] * lax.axis_size(("vgrp", "samp"))), ("vgrp", "samp"), 0, 0
+        ),
+        axis=0,
+    )
     samples = pheno_full.shape[0]
     local_rows = exposures.shape[0]
     width = exposures.shape[1]

time: 588 us -> 772 us (1.31)
  waiting for transfers between devices: 193 us -> 438 us
  blocking collectives: 151 us -> 74.5 us
  starting transfers between devices: 0.04 us -> 14.7 us
    psum x1, waiting for transfers between devices: 0.01 us -> 246 us  [per_device(): gram, cross = lax.psum((gram_part, cross_part), ('vgrp', 'samp'))]
    all_gather x1 -> x0, blocking collectives: 77.2 us -> none  [per_device(): pheno_full = lax.all_gather(phenotype, ('vgrp', 'samp'), axis=0, tiled=True)]
    all_to_all x0 -> x1, starting transfers between devices: none -> 14.6 us  [per_device(): lax.all_to_all(jnp.stack([phenotype] * lax.axis_size(('vgrp', 'samp'))),...]
  transfers between devices with their start and end apart: 2 -> 3, of which waited for: 1 -> 2; matrix products, arithmetic and copies ran while one was open for 31% -> 4% of each run, Pallas kernels for 0% -> 0%
where the time goes in v1:
time: 772 us; the launch traced here: 771 us
  waiting for transfers between devices  438 us (57%)
  local copies, waits for them, and re-layouts  139 us (18%)
  other arithmetic  76.3 us (10%)
  blocking collectives  74.5 us (10%)
  matrix products  15.1 us (2%)
  starting transfers between devices  14.7 us (2%)
  between operations  13.6 us (2%)
    psum x1, waiting for transfers between devices, per_device(): gram, cross = lax.psum((gram_part, cross_part), ('vgrp', 'samp'))  246 us
    psum x1, waiting for transfers between devices, per_device(): lax.psum(jnp.dot(dosages.T, weighted, preferred_element_type=jnp.float32)...  192 us
    gather x16, local copies, waits for them, and re-layouts, one_perm(): picked_rows = table[index_row // 128]  130 us
    psum x1, blocking collectives, per_device(): gram, cross = lax.psum((gram_part, cross_part), ('vgrp', 'samp'))  74.5 us
    reduce_sum x16, other arithmetic, one_perm(): return jnp.sum(jnp.where(wanted, picked_rows, jnp.float32(0.0)), axis=1)  30.2 us
    select_n x16, other arithmetic, one_perm(): picked_rows = table[index_row // 128]  15.6 us
  transfers between devices with their start and end apart: 3, of which 2 were waited for; matrix products, arithmetic and copies ran while one was open for 4% of the time, Pallas kernels for 0%

profile of v1, /device:TPU:8, one launch (start us, length us, event | category | flops | bytes accessed | tf_op | source)
XLA Modules:
  0.0 771.4 jit_solution(2893386217389031496)
XLA Ops:
  6.5 2.1 stack.2
  8.6 14.6 %all-to-all-start = ((f32[256,1,768]{2,1,0:T(1,128)}), f32[256,1,768]{2,1,0:T(1,128)S(1)}, u32[]{:S(2)}, u32[]{:S(2)}) async-start(f32[256,1,768]{2,1,0:T(1,128)} %stack.2), calls=%async_computation | async-start | bytes 1572864 | tf_op jit(solution)/shard_map/all_to_all | solution.py:28
  26.5 245.7 %all-reduce.3.cloned.1.call-done = f32[128,128]{1,0:T(8,128)} async-done(((f32[128,128]{1,0:T(8,128)}), f32[128,128]{1,0:T(8,128)}) %all-reduce.3.cloned.1.call-update) | async-done | bytes 65552 | tf_op jit(solution)/shard_map/psum | solution.py:43
  274.0 11.7 %cholesky.16 = f32[128,128]{1,0:T(8,128)S(1)} custom-call(f32[128,128]{1,0:T(8,128)S(1)} %fusion.14), custom_call_target="Cholesky" | custom-call | tf_op jit(solution)/shard_map/jit(cholesky)/cholesky | solution.py:45
  286.9 9.8 %custom-call.8 = f32[1,128,128]{1,2,0:T(8,128)S(1)} custom-call(f32[1,128,128]{2,1,0:T(8,128)S(1)} %fusion.9), custom_call_target="InvertDiagBlocksLowerTriangular" | custom-call | tf_op jit(solution)/shard_map/triangular_solve | solution.py:9
  296.7 181.6 %while.13 = (s32[]{:T(128)}, f32[16,3072]{1,0:T(8,128)S(1)}, s32[16,3072]{1,0:T(8,128)}, f32[1536,128]{1,0:T(8,128)S(1)}, s32[]{:T(128)}, /*index=5*/s32[]{:T(128)}) while((s32[]{:T(128)}, f32[16,3072]{1,0:T(8,128)S(1)}, s32[16,3072]{1,0:T(8,128)}, f32[1536,128]{1,0:T(8,128)S(1)}, s32[]{:T(128)}, /*index=5*/s32[]{:T(128)}) %tuple.39), condition=%wide.region_2.3_spmd.clone, body=%wide.region_0.2_spmd.clone.sunk | while | flops 1268738 | bytes 4866133 | solution.py:22
  297.8 8.1 %gather_fusion = f32[3072,128]{1,0:T(8,128)S(1)} fusion(f32[1536,128]{1,0:T(8,128)S(1)} %get-tuple-element.138, s32[3072]{0:T(1024)S(1)} %broadcast_clamp_fusion.2), kind=kCustom, calls=%fused_computation.clone.clone.1 | custom fusion | bytes 3158016 | tf_op jit(solution)/shard_map/while/body/eval_jaxpr/gather | solution.py:18
  309.1 8.1 %gather_fusion = f32[3072,128]{1,0:T(8,128)S(1)} fusion(f32[1536,128]{1,0:T(8,128)S(1)} %get-tuple-element.138, s32[3072]{0:T(1024)S(1)} %broadcast_clamp_fusion.2), kind=kCustom, calls=%fused_computation.clone.clone.1 | custom fusion | bytes 3158016 | tf_op jit(solution)/shard_map/while/body/eval_jaxpr/gather | solution.py:18
  320.5 8.1 %gather_fusion = f32[3072,128]{1,0:T(8,128)S(1)} fusion(f32[1536,128]{1,0:T(8,128)S(1)} %get-tuple-element.138, s32[3072]{0:T(1024)S(1)} %broadcast_clamp_fusion.2), kind=kCustom, calls=%fused_computation.clone.clone.1 | custom fusion | bytes 3158016 | tf_op jit(solution)/shard_map/while/body/eval_jaxpr/gather | solution.py:18
  328.6 1.9 select_reduce_fusion.3
  331.8 8.1 %gather_fusion = f32[3072,128]{1,0:T(8,128)S(1)} fusion(f32[1536,128]{1,0:T(8,128)S(1)} %get-tuple-element.138, s32[3072]{0:T(1024)S(1)} %broadcast_clamp_fusion.2), kind=kCustom, calls=%fused_computation.clone.clone.1 | custom fusion | bytes 3158016 | tf_op jit(solution)/shard_map/while/body/eval_jaxpr/gather | solution.py:18
  339.9 1.9 select_reduce_fusion.3
  343.2 8.1 %gather_fusion = f32[3072,128]{1,0:T(8,128)S(1)} fusion(f32[1536,128]{1,0:T(8,128)S(1)} %get-tuple-element.138, s32[3072]{0:T(1024)S(1)} %broadcast_clamp_fusion.2), kind=kCustom, calls=%fused_computation.clone.clone.1 | custom fusion | bytes 3158016 | tf_op jit(solution)/shard_map/while/body/eval_jaxpr/gather | solution.py:18
  351.3 1.9 select_reduce_fusion.3
  354.5 8.1 %gather_fusion = f32[3072,128]{1,0:T(8,128)S(1)} fusion(f32[1536,128]{1,0:T(8,128)S(1)} %get-tuple-element.138, s32[3072]{0:T(1024)S(1)} %broadcast_clamp_fusion.2), kind=kCustom, calls=%fused_computation.clone.clone.1 | custom fusion | bytes 3158016 | tf_op jit(solution)/shard_map/while/body/eval_jaxpr/gather | solution.py:18
  365.9 8.1 %gather_fusion = f32[3072,128]{1,0:T(8,128)S(1)} fusion(f32[1536,128]{1,0:T(8,128)S(1)} %get-tuple-element.138, s32[3072]{0:T(1024)S(1)} %broadcast_clamp_fusion.2), kind=kCustom, calls=%fused_computation.clone.clone.1 | custom fusion | bytes 3158016 | tf_op jit(solution)/shard_map/while/body/eval_jaxpr/gather | solution.py:18
  377.2 8.1 %gather_fusion = f32[3072,128]{1,0:T(8,128)S(1)} fusion(f32[1536,128]{1,0:T(8,128)S(1)} %get-tuple-element.138, s32[3072]{0:T(1024)S(1)} %broadcast_clamp_fusion.2), kind=kCustom, calls=%fused_computation.clone.clone.1 | custom fusion | bytes 3158016 | tf_op jit(solution)/shard_map/while/body/eval_jaxpr/gather | solution.py:18
  385.4 1.9 select_reduce_fusion.3
  388.6 8.1 %gather_fusion = f32[3072,128]{1,0:T(8,128)S(1)} fusion(f32[1536,128]{1,0:T(8,128)S(1)} %get-tuple-element.138, s32[3072]{0:T(1024)S(1)} %broadcast_clamp_fusion.2), kind=kCustom, calls=%fused_computation.clone.clone.1 | custom fusion | bytes 3158016 | tf_op jit(solution)/shard_map/while/body/eval_jaxpr/gather | solution.py:18
  396.7 1.9 select_reduce_fusion.3
  399.9 8.1 %gather_fusion = f32[3072,128]{1,0:T(8,128)S(1)} fusion(f32[1536,128]{1,0:T(8,128)S(1)} %get-tuple-element.138, s32[3072]{0:T(1024)S(1)} %broadcast_clamp_fusion.2), kind=kCustom, calls=%fused_computation.clone.clone.1 | custom fusion | bytes 3158016 | tf_op jit(solution)/shard_map/while/body/eval_jaxpr/gather | solution.py:18
  411.3 8.1 %gather_fusion = f32[3072,128]{1,0:T(8,128)S(1)} fusion(f32[1536,128]{1,0:T(8,128)S(1)} %get-tuple-element.138, s32[3072]{0:T(1024)S(1)} %broadcast_clamp_fusion.2), kind=kCustom, calls=%fused_computation.clone.clone.1 | custom fusion | bytes 3158016 | tf_op jit(solution)/shard_map/while/body/eval_jaxpr/gather | solution.py:18
  422.6 8.1 %gather_fusion = f32[3072,128]{1,0:T(8,128)S(1)} fusion(f32[1536,128]{1,0:T(8,128)S(1)} %get-tuple-element.138, s32[3072]{0:T(1024)S(1)} %broadcast_clamp_fusion.2), kind=kCustom, calls=%fused_computation.clone.clone.1 | custom fusion | bytes 3158016 | tf_op jit(solution)/shard_map/while/body/eval_jaxpr/gather | solution.py:18
  434.0 8.1 %gather_fusion = f32[3072,128]{1,0:T(8,128)S(1)} fusion(f32[1536,128]{1,0:T(8,128)S(1)} %get-tuple-element.138, s32[3072]{0:T(1024)S(1)} %broadcast_clamp_fusion.2), kind=kCustom, calls=%fused_computation.clone.clone.1 | custom fusion | bytes 3158016 | tf_op jit(solution)/shard_map/while/body/eval_jaxpr/gather | solution.py:18
  445.3 8.1 %gather_fusion = f32[3072,128]{1,0:T(8,128)S(1)} fusion(f32[1536,128]{1,0:T(8,128)S(1)} %get-tuple-element.138, s32[3072]{0:T(1024)S(1)} %broadcast_clamp_fusion.2), kind=kCustom, calls=%fused_computation.clone.clone.1 | custom fusion | bytes 3158016 | tf_op jit(solution)/shard_map/while/body/eval_jaxpr/gather | solution.py:18
  456.7 8.1 %gather_fusion = f32[3072,128]{1,0:T(8,128)S(1)} fusion(f32[1536,128]{1,0:T(8,128)S(1)} %get-tuple-element.138, s32[3072]{0:T(1024)S(1)} %broadcast_clamp_fusion.2), kind=kCustom, calls=%fused_computation.clone.clone.1 | custom fusion | bytes 3158016 | tf_op jit(solution)/shard_map/while/body/eval_jaxpr/gather | solution.py:18
  468.0 8.1 %gather_fusion = f32[3072,128]{1,0:T(8,128)S(1)} fusion(f32[1536,128]{1,0:T(8,128)S(1)} %get-tuple-element.138, s32[3072]{0:T(1024)S(1)} %broadcast_clamp_fusion.2), kind=kCustom, calls=%fused_computation.clone.clone.1 | custom fusion | bytes 3158016 | tf_op jit(solution)/shard_map/while/body/eval_jaxpr/gather | solution.py:18
  479.8 74.5 %psum.22 = f32[128,16]{0,1:T(8,128)S(1)} all-reduce(f32[128,16]{0,1:T(8,128)S(1)} %fusion.5), channel_id=1, replica_groups=mesh['vgrp'=4,'samp'=64] {'vgrp','samp'}, use_global_device_ids=true, to_apply=%region_6.7 | all-reduce | flops 2048 | bytes 16384 | tf_op jit(solution)/shard_map/psum | solution.py:43
  554.6 3.0 fusion.3
  557.7 3.4 multiply_convert_fusion
  561.1 8.9 %convolution_bitcast_fusion = f32[512,2048]{0,1:T(8,128)} fusion(bf16[3072,2048]{0,1:T(8,128)(2,1)S(1)} %bitcast.45, s32[3072,512]{1,0:T(8,128)S(1)} %bitcast.51), kind=kOutput, calls=%fused_computation.19 | convolution fusion | flops 6444023808 | bytes 23068672 | tf_op jit(solution)/shard_map/dot_general | solution.py:57
  570.1 192.1 %all-reduce.5.cloned.1.call-done = f32[512,2048]{0,1:T(8,128)} async-done(((f32[512,2048]{0,1:T(8,128)}), f32[512,2048]{0,1:T(8,128)}) %all-reduce.5.cloned.1.call-update) | async-done | bytes 4194320 | tf_op jit(solution)/shard_map/psum | solution.py:57
  (105 shorter events, 51.8 us)
Async XLA Ops:
  6.5 16.8 %copy-start = (f32[3072,128]{1,0:T(8,128)S(1)}, f32[3072,128]{1,0:T(8,128)}, u32[]{:S(2)}) copy-start(f32[3072,128]{1,0:T(8,128)} %param.7) | copy-start | bytes 4718596
  8.6 288.1 %all-to-all-start = ((f32[256,1,768]{2,1,0:T(1,128)}), f32[256,1,768]{2,1,0:T(1,128)S(1)}, u32[]{:S(2)}, u32[]{:S(2)}) async-start(f32[256,1,768]{2,1,0:T(1,128)} %stack.2), calls=%async_computation | async-start | bytes 1572864 | tf_op jit(solution)/shard_map/all_to_all | solution.py:28
  23.3 248.9 %all-reduce.3.cloned.1.call-start = ((), (), s32[]{:S(2)}) async-start(), calls=%async_computation.1 | async-start | bytes 131072 | tf_op jit(solution)/shard_map/psum | solution.py:43
  24.8 737.4 %all-reduce.5.cloned.1.call-start = ((), (), s32[]{:S(2)}) async-start(), calls=%async_computation.2 | async-start | bytes 8388608 | tf_op jit(solution)/shard_map/psum | solution.py:57
  478.4 79.2 %copy-start.1 = (f32[3072,128]{0,1:T(8,128)S(1)}, f32[3072,128]{0,1:T(8,128)}, u32[]{:S(2)}) copy-start(f32[3072,128]{0,1:T(8,128)} %copy.12) | copy-start | bytes 4718596
  554.6 6.5 slice-start
  557.6 3.5 slice-start.1
Sparse Core Ops, SparseCore 0:
  29.6 242.5 all-reduce.2
  570.2 191.9 all-reduce.4
